TPU v7x, 512 devices: a whole 4x8x8 slice. The times are simulated.
512 devices in a mesh: sub: 32 (over x_lo, z, core), grp: 16 (over x_hi, y).
Axes of the slice: x: 4 (x_hi: 2, x_lo: 2; x = x_hi * 2 + x_lo), y: 8, z: 8, core: 2. Of those that a mesh axis runs over, the one named last changes fastest.
Arguments:
- deflation: bfloat16 [32, 3, 512, 128, 128], P(None, None, 'sub', 'grp'), may hold values from -10 to 10, as said below
- stiffness: bfloat16 [4, 512, 128, 128], P(None, 'sub', 'grp'), may hold values from 0.02 to 40, as said below
- depths: int32 [512], P(('sub', 'grp')), may hold values from 1 to 128, 49152 in all
Outputs:
- coarse_rows: float32 [32, 16, 32, 96], P('sub')
Inputs may be any that keep to these rules, and one draw needn't show every extreme that they name: `deflation`: entries of order one. `stiffness`: positive coefficients. `depths`: the deepest subdomain has all 128 cells live.
All inputs are finite; a program needn't handle non-finite values. No bound on the sum of `depths` on one device may be relied on, other than what follows from the above.
Results may differ from a plain program's by a relative error of at most 0.0003.
Values may be sent and summed in bfloat16 or wider, within the bound.
No kernel may reach another device: no remote copies, remote signals or barrier semaphores. Data moves between devices by JAX's collectives and lax.ppermute only.
A program may use at most 128 MiB of HBM per device.

v0:
```python
import jax
import jax.numpy as jnp
from jax import lax
from jax.sharding import PartitionSpec as P


def from_behind(x, axis, by):
    length = lax.axis_size(axis)
    pairs = [(i, i + by) for i in range(length) if 0 <= i + by < length]
    return lax.ppermute(x, axis, pairs)


def gram_of(left_side, right_side):
    count = left_side.shape[0]
    return jnp.dot(
        left_side.reshape(count, -1),
        right_side.reshape(count, -1).T,
        preferred_element_type=jnp.float32,
    )


def weighted(weight, values):
    return (weight.astype(jnp.float32) * values.astype(jnp.float32)).astype(jnp.bfloat16)


def differences(values, dim_index):
    widened = values.astype(jnp.float32)
    length = widened.shape[dim_index]
    following = jnp.concatenate(
        [
            lax.slice_in_dim(widened, 1, length, axis=dim_index),
            jnp.zeros_like(lax.slice_in_dim(widened, 0, 1, axis=dim_index)),
        ],
        axis=dim_index,
    )
    return (widened - following).astype(jnp.bfloat16)


def local_terms(live_field, coefficients):
    accumulated = gram_of(live_field, weighted(coefficients[0], live_field))
    for entry in range(3):
        stepped = differences(live_field, entry + 2)
        accumulated = accumulated + gram_of(stepped, weighted(coefficients[entry + 1], stepped))
    return accumulated


def shards(deflation, stiffness, depths):
    cell_count = deflation.shape[2] * deflation.shape[3] * deflation.shape[4]
    normalizer = 1.0 / (24.0 * cell_count)
    live_mask = (lax.iota(jnp.int32, deflation.shape[4]) < depths[0]).astype(jnp.bfloat16)
    live_field = deflation * live_mask
    diagonal_block = local_terms(live_field, stiffness)
    top_x = live_field[:, :, -1]
    bottom_x = live_field[:, :, 0]
    weight_top_x = stiffness[1, -1]
    next_x = from_behind(bottom_x, "sub", -1)
    coupling_x = -gram_of(weighted(weight_top_x, top_x), next_x)
    face_term = gram_of(next_x, weighted(weight_top_x, next_x))
    lower_x = from_behind(face_term, "sub", 1)
    diagonal_block = diagonal_block + lower_x
    bottom_y = live_field[:, :, :, 0]
    weight_top_y = stiffness[2, :, -1]
    next_y = from_behind(bottom_y, "grp", -1)
    weight_low_y = from_behind(weight_top_y, "grp", 1)
    diagonal_block = diagonal_block + gram_of(bottom_y, weighted(weight_low_y, bottom_y))
    coupling_y = -gram_of(weighted(weight_top_y, live_field[:, :, :, -1]), next_y)
    row_block = normalizer * jnp.concatenate([diagonal_block, coupling_x, coupling_y], axis=1)
    return lax.all_gather(row_block[None, None], "grp", axis=1, tiled=True)


def solution(mesh):
    in_specs = (P(None, None, "sub", "grp", None), P(None, "sub", "grp", None), P(("sub", "grp")))
    out_specs = P("sub", None, None, None)
    return jax.shard_map(shards, mesh=mesh, in_specs=in_specs, out_specs=out_specs, check_vma=False)
```

profile of v0, /device:TPU:2, one launch (start us, length us, event | category | flops | bytes accessed | tf_op | source)
XLA Modules:
  0.0 105.4 jit_solution(15280825005196992566)
XLA Ops:
  0.0 0.8 slice.49
  0.8 3.5 %collective-permute-start.2 = (bf16[16,128]{1,0:T(8,128)(2,1)S(1)}, bf16[16,128]{1,0:T(8,128)(2,1)S(1)}, u32[]{:S(2)}, u32[]{:S(2)}) collective-permute-start(bf16[16,128]{1,0:T(8,128)(2,1)S(1)} %get-tuple-element.14), channel_id=1, source_target_pairs={{0,1},{1,2},{2,3},{3,4},{4,5},{5,6},{6,7},{7,8},{8,9},{9,10},{10,1... | collective-permute-start | bytes 12296 | tf_op jit(solution)/shard_map/ppermute | solution.py:10
  4.3 0.8 bitcast_convert_fusion
  5.8 6.2 %multiply_convert_fusion.3 = (bf16[32,3,16,8,128]{4,0,3,1,2:T(8,128)(2,1)S(1)}, bf16[32,3,16,8,128]{4,0,3,1,2:T(8,128)(2,1)S(1)}) fusion(f32[16,8,128]{2,1,0:T(8,128)S(1)} %get-tuple-element.22, bf16[128]{0:T(256)(128)(2,1)S(1)} %compare_convert_fusion, bf16[32,3,16,8,128]{4,3,2,1,0:T(8,128)(2,1)} %param.3), kind=kLoop, calls=%fused_computation.6 | loop fusion | flops 6291456 | bytes 9502976 | tf_op jit(solution)/shard_map/convert_element_type | solution.py:23
  12.0 10.1 %collective-permute-start = (bf16[32,3,8,128]{3,0,2,1:T(8,128)(2,1)S(1)}, bf16[32,3,8,128]{3,0,2,1:T(8,128)(2,1)S(1)}, u32[]{:S(2)}, u32[]{:S(2)}) collective-permute-start(bf16[32,3,8,128]{3,0,2,1:T(8,128)(2,1)S(1)} %slice_bitcast_fusion.4), channel_id=1, source_target_pairs={{16,0},{32,16},{48,32},{64,48},{80,64},{96,80},{112,96},{128,112},... | collective-permute-start | bytes 589832 | tf_op jit(solution)/shard_map/ppermute | solution.py:10
  22.1 1.5 %collective-permute-start.3 = (bf16[32,3,16,128]{3,0,1,2:T(8,128)(2,1)S(1)}, bf16[32,3,16,128]{3,0,1,2:T(8,128)(2,1)S(1)}, u32[]{:S(2)}, u32[]{:S(2)}) collective-permute-start(bf16[32,3,16,128]{3,0,1,2:T(8,128)(2,1)S(1)} %slice_bitcast_fusion.1), channel_id=1, source_target_pairs={{1,0},{2,1},{3,2},{4,3},{5,4},{6,5},{7,6},{8,7},{9,8},{10,9},{11,1... | collective-permute-start | bytes 1179656 | tf_op jit(solution)/shard_map/ppermute | solution.py:10
  23.6 3.2 %slice.53 = f32[32,3,16,7,128]{4,0,3,1,2:T(8,128)} slice(bf16[32,3,16,8,128]{4,0,3,1,2:T(8,128)(2,1)S(1)} %get-tuple-element.12), slice={[0:32], [0:3], [0:16], [1:8], [0:128]} | slice | bytes 11010048 | tf_op jit(solution)/shard_map/slice | solution.py:31
  26.8 3.4 %slice.52 = f32[32,3,15,8,128]{4,0,3,1,2:T(8,128)} slice(bf16[32,3,16,8,128]{4,0,3,1,2:T(8,128)(2,1)S(1)} %get-tuple-element.12), slice={[0:32], [0:3], [1:16], [0:8], [0:128]} | slice | bytes 11796480 | tf_op jit(solution)/shard_map/slice | solution.py:31
  30.1 1.0 slice.54
  31.2 0.9 fusion.12
  32.1 12.0 %multiply_convert_fusion = (bf16[32,3,16,8,128]{4,0,3,1,2:T(8,128)(2,1)}, bf16[32,3,16,8,128]{4,0,3,1,2:T(8,128)(2,1)}, bf16[32,3,16,8,128]{4,0,3,1,2:T(8,128)(2...) fusion(f32[16,8,128]{2,1,0:T(8,128)S(1)} %get-tuple-element.19,, ...), kind=kLoop, calls=%fused_computation | loop fusion | flops 25165824 | bytes 39862272 | tf_op jit(solution)/shard_map/convert_element_type | solution.py:23
  44.1 0.0 copy-start.2
  44.1 3.9 %fusion.46 = f32[32,32]{1,0:T(8,128)S(1)} fusion(f32[32,32]{1,0:T(8,128)S(1)} %fusion.12, bf16[32,3,16,8,128]{4,0,3,1,2:T(8,128)(2,1)} %get-tuple-element.15, bf16[32,3,16,8,128]{4,0,3,1,2:T(8,128)(2,1)} %get-tuple-element.16), kind=kOutput, calls=%fused_computation.34 | convolution fusion | flops 100664320 | bytes 6299648 | tf_op jit(solution)/shard_map/dot_general | solution.py:15
  48.1 0.0 copy-done.2
  48.1 0.7 copy-done.3
  48.8 1.0 fusion.41
  49.8 0.9 copy-done
  50.7 1.0 copy-done.1
  51.7 1.0 fusion.36
  52.6 0.7 bitcast_convert_fusion.4
  53.3 0.0 collective-permute-done.2
  53.3 0.0 collective-permute-done
  53.3 0.2 convolution_bitcast_fusion.3
  53.5 1.9 %collective-permute-start.1 = (f32[32,32]{1,0:T(8,128)S(1)}, f32[32,32]{1,0:T(8,128)S(1)}, u32[]{:S(2)}, u32[]{:S(2)}) collective-permute-start(f32[32,32]{1,0:T(8,128)S(1)} %convolution_bitcast_fusion.3), channel_id=1, source_target_pairs={{0,16},{16,32},{32,48},{48,64},{64,80},{80,96},{96,112},{112,128},... | collective-permute-start | bytes 12296 | tf_op jit(solution)/shard_map/ppermute | solution.py:10
  55.5 0.2 fusion.35
  55.6 5.1 %collective-permute-done.1 = f32[32,32]{1,0:T(8,128)S(1)} collective-permute-done((f32[32,32]{1,0:T(8,128)S(1)}, f32[32,32]{1,0:T(8,128)S(1)}, u32[]{:S(2)}, u32[]{:S(2)}) %collective-permute-start.1) | collective-permute-done | bytes 4128 | tf_op jit(solution)/shard_map/ppermute | solution.py:10
  60.7 0.2 add_bitcast_fusion
  60.9 0.0 collective-permute-done.3
  61.0 0.2 fusion.33
  61.2 0.1 fusion.61
  61.3 43.4 %all_gather.3 = f32[1,16,32,96]{3,2,0,1:T(8,128)S(1)} all-gather(f32[1,1,32,96]{3,2,0,1:T(8,128)S(1)} %fusion.61), channel_id=1, replica_groups=mesh['sub'=32,'grp'=16] {'grp'}, dimensions={1}, use_global_device_ids=true | all-gather | bytes 208896 | tf_op jit(solution)/shard_map/all_gather | solution.py:68
  104.7 0.7 copy.118
  (8 shorter events, 0.1 us)
Async XLA Ops:
  0.8 52.5 %collective-permute-start.2 = (bf16[16,128]{1,0:T(8,128)(2,1)S(1)}, bf16[16,128]{1,0:T(8,128)(2,1)S(1)}, u32[]{:S(2)}, u32[]{:S(2)}) collective-permute-start(bf16[16,128]{1,0:T(8,128)(2,1)S(1)} %get-tuple-element.14), channel_id=1, source_target_pairs={{0,1},{1,2},{2,3},{3,4},{4,5},{5,6},{6,7},{7,8},{8,9},{9,10},{10,1... | collective-permute-start | bytes 12296 | tf_op jit(solution)/shard_map/ppermute | solution.py:10
  12.0 41.4 %collective-permute-start = (bf16[32,3,8,128]{3,0,2,1:T(8,128)(2,1)S(1)}, bf16[32,3,8,128]{3,0,2,1:T(8,128)(2,1)S(1)}, u32[]{:S(2)}, u32[]{:S(2)}) collective-permute-start(bf16[32,3,8,128]{3,0,2,1:T(8,128)(2,1)S(1)} %slice_bitcast_fusion.4), channel_id=1, source_target_pairs={{16,0},{32,16},{48,32},{64,48},{80,64},{96,80},{112,96},{128,112},... | collective-permute-start | bytes 589832 | tf_op jit(solution)/shard_map/ppermute | solution.py:10
  22.1 38.9 %collective-permute-start.3 = (bf16[32,3,16,128]{3,0,1,2:T(8,128)(2,1)S(1)}, bf16[32,3,16,128]{3,0,1,2:T(8,128)(2,1)S(1)}, u32[]{:S(2)}, u32[]{:S(2)}) collective-permute-start(bf16[32,3,16,128]{3,0,1,2:T(8,128)(2,1)S(1)} %slice_bitcast_fusion.1), channel_id=1, source_target_pairs={{1,0},{2,1},{3,2},{4,3},{5,4},{6,5},{7,6},{8,7},{9,8},{10,9},{11,1... | collective-permute-start | bytes 1179656 | tf_op jit(solution)/shard_map/ppermute | solution.py:10
  44.1 4.0 %copy-start.2 = (bf16[32,3,16,8,128]{4,0,3,1,2:T(8,128)(2,1)S(1)}, bf16[32,3,16,8,128]{4,0,3,1,2:T(8,128)(2,1)}, u32[]{:S(2)}) copy-start(bf16[32,3,16,8,128]{4,0,3,1,2:T(8,128)(2,1)} %get-tuple-element.17) | copy-start | bytes 9437188
  44.1 4.7 %copy-start.3 = (bf16[32,3,16,8,128]{4,0,3,1,2:T(8,128)(2,1)S(1)}, bf16[32,3,16,8,128]{4,0,3,1,2:T(8,128)(2,1)}, u32[]{:S(2)}) copy-start(bf16[32,3,16,8,128]{4,0,3,1,2:T(8,128)(2,1)} %get-tuple-element.18) | copy-start | bytes 9437188
  48.8 1.9 %copy-start = (bf16[32,3,16,8,128]{4,0,3,1,2:T(8,128)(2,1)S(1)}, bf16[32,3,16,8,128]{4,0,3,1,2:T(8,128)(2,1)}, u32[]{:S(2)}) copy-start(bf16[32,3,16,8,128]{4,0,3,1,2:T(8,128)(2,1)} %get-tuple-element.5) | copy-start | bytes 9437188
  48.8 2.8 %copy-start.1 = (bf16[32,3,16,8,128]{4,0,3,1,2:T(8,128)(2,1)S(1)}, bf16[32,3,16,8,128]{4,0,3,1,2:T(8,128)(2,1)}, u32[]{:S(2)}) copy-start(bf16[32,3,16,8,128]{4,0,3,1,2:T(8,128)(2,1)} %get-tuple-element.6) | copy-start | bytes 9437188
  53.5 7.2 %collective-permute-start.1 = (f32[32,32]{1,0:T(8,128)S(1)}, f32[32,32]{1,0:T(8,128)S(1)}, u32[]{:S(2)}, u32[]{:S(2)}) collective-permute-start(f32[32,32]{1,0:T(8,128)S(1)} %convolution_bitcast_fusion.3), channel_id=1, source_target_pairs={{0,16},{16,32},{32,48},{48,64},{64,80},{80,96},{96,112},{112,128},... | collective-permute-start | bytes 12296 | tf_op jit(solution)/shard_map/ppermute | solution.py:10
where the time goes:
time: 106 us; the launch traced here: 105 us
  blocking collectives  43.4 us (41%)
  other arithmetic  19.8 us (19%)
  starting transfers between devices  17 us (16%)
  local copies, waits for them, and re-layouts  11.7 us (11%)
  matrix products  7.63 us (7%)
  waiting for transfers between devices  5.07 us (5%)
    all_gather x1, blocking collectives, shards(): return lax.all_gather(row_block[None, None], 'grp', axis=1, tiled=True)  43.4 us
    convert_element_type x2, other arithmetic, weighted(): (weight.astype(jnp.float32) * values.astype(jnp.float32)).astype(jnp.bflo...  18.2 us
    ppermute x4, starting transfers between devices, from_behind(): return lax.ppermute(x, axis, pairs)  17 us
    dot_general x8, matrix products, gram_of(): jnp.dot(left_side.reshape(count, -1), right_side.reshape(count, -1).T, pr...  7.63 us
    slice x3, local copies, waits for them, and re-layouts, differences(): lax.slice_in_dim(widened, 1, length, axis=dim_index)  7.61 us
    ppermute x4, waiting for transfers between devices, from_behind(): return lax.ppermute(x, axis, pairs)  5.07 us
    unnamed x9, local copies, waits for them, and re-layouts  3.33 us
  transfers between devices with their start and end apart: 4, of which 1 were waited for; matrix products, arithmetic and copies ran while one was open for 33% of the time, Pallas kernels for 0%

commit v1 on v0

--- a/solution.py
+++ b/solution.py
@@ -65,7 +65,16 @@
     diagonal_block = diagonal_block + gram_of(bottom_y, weighted(weight_low_y, bottom_y))
     coupling_y = -gram_of(weighted(weight_top_y, live_field[:, :, :, -1]), next_y)
     row_block = normalizer * jnp.concatenate([diagonal_block, coupling_x, coupling_y], axis=1)
-    return lax.all_gather(row_block[None, None], "grp", axis=1, tiled=True)
+
+    def hold_lanes(unit):
+        return jnp.concatenate(
+            jax.lax.all_to_all(
+                jnp.stack([unit for _ in range(jax.lax.axis_size("grp"))], axis=0), "grp", 0, 0
+            ),
+            1,
+        )
+
+    return hold_lanes(row_block[None, None])
 
 
 def solution(mesh):

time: 106 us -> 84.5 us (0.80)
  the two profiles are of different devices: /device:TPU:2 before, /device:TPU:10 now
where the time goes in v1:
time: 84.5 us; the launch traced here: 84.1 us
  blocking collectives  21 us (25%)
  other arithmetic  19.8 us (23%)
  starting transfers between devices  18 us (21%)
  local copies, waits for them, and re-layouts  11.8 us (14%)
  matrix products  7.64 us (9%)
  waiting for transfers between devices  5.07 us (6%)
    all_to_all x1, blocking collectives, hold_lanes(): jax.lax.all_to_all(jnp.stack([unit for _ in range(jax.lax.axis_size('grp'...  21 us
    convert_element_type x2, other arithmetic, weighted(): (weight.astype(jnp.float32) * values.astype(jnp.float32)).astype(jnp.bflo...  18.2 us
    ppermute x4, starting transfers between devices, from_behind(): return lax.ppermute(x, axis, pairs)  18 us
    dot_general x8, matrix products, gram_of(): jnp.dot(left_side.reshape(count, -1), right_side.reshape(count, -1).T, pr...  7.64 us
    slice x3, local copies, waits for them, and re-layouts, differences(): lax.slice_in_dim(widened, 1, length, axis=dim_index)  7.61 us
    ppermute x4, waiting for transfers between devices, from_behind(): return lax.ppermute(x, axis, pairs)  5.07 us
    unnamed x9, local copies, waits for them, and re-layouts  3.32 us
  transfers between devices with their start and end apart: 4, of which 1 were waited for; matrix products, arithmetic and copies ran while one was open for 41% of the time, Pallas kernels for 0%

profile of v1, /device:TPU:10, one launch (start us, length us, event | category | flops | bytes accessed | tf_op | source)
XLA Modules:
  0.0 84.1 jit_solution(6211183032656931725)
XLA Ops:
  0.0 0.8 slice.49
  0.8 3.5 %collective-permute-start.2 = (bf16[16,128]{1,0:T(8,128)(2,1)S(1)}, bf16[16,128]{1,0:T(8,128)(2,1)S(1)}, u32[]{:S(2)}, u32[]{:S(2)}) collective-permute-start(bf16[16,128]{1,0:T(8,128)(2,1)S(1)} %get-tuple-element.14), channel_id=1, source_target_pairs={{0,1},{1,2},{2,3},{3,4},{4,5},{5,6},{6,7},{7,8},{8,9},{9,10},{10,1... | collective-permute-start | bytes 12296 | tf_op jit(solution)/shard_map/ppermute | solution.py:10
  4.3 0.8 bitcast_convert_fusion
  5.8 6.2 %multiply_convert_fusion.3 = (bf16[32,3,16,8,128]{4,0,3,1,2:T(8,128)(2,1)S(1)}, bf16[32,3,16,8,128]{4,0,3,1,2:T(8,128)(2,1)S(1)}) fusion(f32[16,8,128]{2,1,0:T(8,128)S(1)} %get-tuple-element.22, bf16[128]{0:T(256)(128)(2,1)S(1)} %compare_convert_fusion, bf16[32,3,16,8,128]{4,3,2,1,0:T(8,128)(2,1)} %param.3), kind=kLoop, calls=%fused_computation.6 | loop fusion | flops 6291456 | bytes 9502976 | tf_op jit(solution)/shard_map/convert_element_type | solution.py:23
  12.0 10.1 %collective-permute-start = (bf16[32,3,8,128]{3,0,2,1:T(8,128)(2,1)S(1)}, bf16[32,3,8,128]{3,0,2,1:T(8,128)(2,1)S(1)}, u32[]{:S(2)}, u32[]{:S(2)}) collective-permute-start(bf16[32,3,8,128]{3,0,2,1:T(8,128)(2,1)S(1)} %slice_bitcast_fusion.4), channel_id=1, source_target_pairs={{16,0},{32,16},{48,32},{64,48},{80,64},{96,80},{112,96},{128,112},... | collective-permute-start | bytes 589832 | tf_op jit(solution)/shard_map/ppermute | solution.py:10
  22.1 2.5 %collective-permute-start.3 = (bf16[32,3,16,128]{3,0,1,2:T(8,128)(2,1)S(1)}, bf16[32,3,16,128]{3,0,1,2:T(8,128)(2,1)S(1)}, u32[]{:S(2)}, u32[]{:S(2)}) collective-permute-start(bf16[32,3,16,128]{3,0,1,2:T(8,128)(2,1)S(1)} %slice_bitcast_fusion.1), channel_id=1, source_target_pairs={{1,0},{2,1},{3,2},{4,3},{5,4},{6,5},{7,6},{8,7},{9,8},{10,9},{11,1... | collective-permute-start | bytes 1179656 | tf_op jit(solution)/shard_map/ppermute | solution.py:10
  24.6 3.2 %slice.53 = f32[32,3,16,7,128]{4,0,3,1,2:T(8,128)} slice(bf16[32,3,16,8,128]{4,0,3,1,2:T(8,128)(2,1)S(1)} %get-tuple-element.12), slice={[0:32], [0:3], [0:16], [1:8], [0:128]} | slice | bytes 11010048 | tf_op jit(solution)/shard_map/slice | solution.py:31
  27.9 3.4 %slice.52 = f32[32,3,15,8,128]{4,0,3,1,2:T(8,128)} slice(bf16[32,3,16,8,128]{4,0,3,1,2:T(8,128)(2,1)S(1)} %get-tuple-element.12), slice={[0:32], [0:3], [1:16], [0:8], [0:128]} | slice | bytes 11796480 | tf_op jit(solution)/shard_map/slice | solution.py:31
  31.2 1.0 %slice.54 = f32[32,3,16,8,127]{4,0,3,1,2:T(8,128)S(1)} slice(bf16[32,3,16,8,128]{4,0,3,1,2:T(8,128)(2,1)S(1)} %get-tuple-element.12), slice={[0:32], [0:3], [0:16], [0:8], [1:128]} | slice | bytes 12484608 | tf_op jit(solution)/shard_map/slice | solution.py:31
  32.3 0.9 %fusion.12 = f32[32,32]{1,0:T(8,128)S(1)} fusion(bf16[32,3,16,8,128]{4,0,3,1,2:T(8,128)(2,1)S(1)} %get-tuple-element.11, bf16[32,3,16,8,128]{4,0,3,1,2:T(8,128)(2,1)S(1)} %get-tuple-element.12), kind=kOutput, calls=%fused_computation.20 | convolution fusion | flops 100663296 | bytes 6295552 | tf_op jit(solution)/shard_map/dot_general | solution.py:15
  33.2 12.0 %multiply_convert_fusion = (bf16[32,3,16,8,128]{4,0,3,1,2:T(8,128)(2,1)}, bf16[32,3,16,8,128]{4,0,3,1,2:T(8,128)(2,1)}, bf16[32,3,16,8,128]{4,0,3,1,2:T(8,128)(2...) fusion(f32[16,8,128]{2,1,0:T(8,128)S(1)} %get-tuple-element.19,, ...), kind=kLoop, calls=%fused_computation | loop fusion | flops 25165824 | bytes 39862272 | tf_op jit(solution)/shard_map/convert_element_type | solution.py:23
  45.2 0.0 copy-start.3
  45.2 3.9 %fusion.44 = f32[32,32]{1,0:T(8,128)S(1)} fusion(f32[32,32]{1,0:T(8,128)S(1)} %fusion.12, bf16[32,3,16,8,128]{4,0,3,1,2:T(8,128)(2,1)} %get-tuple-element.15, bf16[32,3,16,8,128]{4,0,3,1,2:T(8,128)(2,1)} %get-tuple-element.16), kind=kOutput, calls=%fused_computation.32 | convolution fusion | flops 100664320 | bytes 6299648 | tf_op jit(solution)/shard_map/dot_general | solution.py:15
  49.1 0.0 copy-done.2
  49.2 0.7 copy-done.3
  49.9 1.0 %fusion.39 = f32[32,32]{1,0:T(8,128)S(1)} fusion(f32[32,32]{1,0:T(8,128)S(1)} %fusion.44, bf16[32,3,16,8,128]{4,0,3,1,2:T(8,128)(2,1)S(1)} %copy-done.2, bf16[32,3,16,8,128]{4,0,3,1,2:T(8,128)(2,1)S(1)} %copy-done.3), kind=kOutput, calls=%fused_computation.31 | convolution fusion | flops 100664320 | bytes 6299648 | tf_op jit(solution)/shard_map/dot_general | solution.py:15
  50.9 0.9 %copy-done = bf16[32,3,16,8,128]{4,0,3,1,2:T(8,128)(2,1)S(1)} copy-done((bf16[32,3,16,8,128]{4,0,3,1,2:T(8,128)(2,1)S(1)}, bf16[32,3,16,8,128]{4,0,3,1,2:T(8,128)(2,1)}, u32[]{:S(2)}) %copy-start) | copy-done | bytes 3145752
  51.8 1.0 %copy-done.1 = bf16[32,3,16,8,128]{4,0,3,1,2:T(8,128)(2,1)S(1)} copy-done((bf16[32,3,16,8,128]{4,0,3,1,2:T(8,128)(2,1)S(1)}, bf16[32,3,16,8,128]{4,0,3,1,2:T(8,128)(2,1)}, u32[]{:S(2)}) %copy-start.1) | copy-done | bytes 3145752
  52.7 1.0 %fusion.34 = f32[32,32]{1,0:T(8,128)S(1)} fusion(f32[32,32]{1,0:T(8,128)S(1)} %fusion.39, bf16[32,3,16,8,128]{4,0,3,1,2:T(8,128)(2,1)S(1)} %copy-done, bf16[32,3,16,8,128]{4,0,3,1,2:T(8,128)(2,1)S(1)} %copy-done.1), kind=kOutput, calls=%fused_computation.30 | convolution fusion | flops 100664320 | bytes 6299648 | tf_op jit(solution)/shard_map/dot_general | solution.py:15
  53.7 0.7 bitcast_convert_fusion.4
  54.4 0.0 collective-permute-done.2
  54.4 0.0 collective-permute-done
  54.4 0.2 convolution_bitcast_fusion.3
  54.6 1.9 %collective-permute-start.1 = (f32[32,32]{1,0:T(8,128)S(1)}, f32[32,32]{1,0:T(8,128)S(1)}, u32[]{:S(2)}, u32[]{:S(2)}) collective-permute-start(f32[32,32]{1,0:T(8,128)S(1)} %convolution_bitcast_fusion.3), channel_id=1, source_target_pairs={{0,16},{16,32},{32,48},{48,64},{64,80},{80,96},{96,112},{112,128},... | collective-permute-start | bytes 12296 | tf_op jit(solution)/shard_map/ppermute | solution.py:10
  56.5 0.2 fusion.33
  56.7 5.1 %collective-permute-done.1 = f32[32,32]{1,0:T(8,128)S(1)} collective-permute-done((f32[32,32]{1,0:T(8,128)S(1)}, f32[32,32]{1,0:T(8,128)S(1)}, u32[]{:S(2)}, u32[]{:S(2)}) %collective-permute-start.1) | collective-permute-done | bytes 4128 | tf_op jit(solution)/shard_map/ppermute | solution.py:10
  61.8 0.2 add_add_fusion
  62.0 0.0 collective-permute-done.3
  62.0 0.2 fusion.32
  62.3 0.1 maximum_multiply_fusion
  62.4 21.0 %all_to_all.5 = f32[16,1,1,32,96]{4,3,2,1,0:T(8,128)S(1)} all-to-all(f32[16,1,1,32,96]{4,3,2,1,0:T(8,128)S(1)} %stack.3), channel_id=1, replica_groups=mesh['sub'=32,'grp'=16] {'grp'}, dimensions={0} | all-to-all | bytes 393216 | tf_op jit(solution)/shard_map/all_to_all | solution.py:71
  83.4 0.7 copy.116
  (9 shorter events, 0.1 us)
Async XLA Ops:
  0.8 53.6 %collective-permute-start.2 = (bf16[16,128]{1,0:T(8,128)(2,1)S(1)}, bf16[16,128]{1,0:T(8,128)(2,1)S(1)}, u32[]{:S(2)}, u32[]{:S(2)}) collective-permute-start(bf16[16,128]{1,0:T(8,128)(2,1)S(1)} %get-tuple-element.14), channel_id=1, source_target_pairs={{0,1},{1,2},{2,3},{3,4},{4,5},{5,6},{6,7},{7,8},{8,9},{9,10},{10,1... | collective-permute-start | bytes 12296 | tf_op jit(solution)/shard_map/ppermute | solution.py:10
  12.0 42.4 %collective-permute-start = (bf16[32,3,8,128]{3,0,2,1:T(8,128)(2,1)S(1)}, bf16[32,3,8,128]{3,0,2,1:T(8,128)(2,1)S(1)}, u32[]{:S(2)}, u32[]{:S(2)}) collective-permute-start(bf16[32,3,8,128]{3,0,2,1:T(8,128)(2,1)S(1)} %slice_bitcast_fusion.4), channel_id=1, source_target_pairs={{16,0},{32,16},{48,32},{64,48},{80,64},{96,80},{112,96},{128,112},... | collective-permute-start | bytes 589832 | tf_op jit(solution)/shard_map/ppermute | solution.py:10
  22.1 39.9 %collective-permute-start.3 = (bf16[32,3,16,128]{3,0,1,2:T(8,128)(2,1)S(1)}, bf16[32,3,16,128]{3,0,1,2:T(8,128)(2,1)S(1)}, u32[]{:S(2)}, u32[]{:S(2)}) collective-permute-start(bf16[32,3,16,128]{3,0,1,2:T(8,128)(2,1)S(1)} %slice_bitcast_fusion.1), channel_id=1, source_target_pairs={{1,0},{2,1},{3,2},{4,3},{5,4},{6,5},{7,6},{8,7},{9,8},{10,9},{11,1... | collective-permute-start | bytes 1179656 | tf_op jit(solution)/shard_map/ppermute | solution.py:10
  45.2 4.0 %copy-start.2 = (bf16[32,3,16,8,128]{4,0,3,1,2:T(8,128)(2,1)S(1)}, bf16[32,3,16,8,128]{4,0,3,1,2:T(8,128)(2,1)}, u32[]{:S(2)}) copy-start(bf16[32,3,16,8,128]{4,0,3,1,2:T(8,128)(2,1)} %get-tuple-element.17) | copy-start | bytes 9437188
  45.2 4.7 %copy-start.3 = (bf16[32,3,16,8,128]{4,0,3,1,2:T(8,128)(2,1)S(1)}, bf16[32,3,16,8,128]{4,0,3,1,2:T(8,128)(2,1)}, u32[]{:S(2)}) copy-start(bf16[32,3,16,8,128]{4,0,3,1,2:T(8,128)(2,1)} %get-tuple-element.18) | copy-start | bytes 9437188
  49.9 1.9 %copy-start = (bf16[32,3,16,8,128]{4,0,3,1,2:T(8,128)(2,1)S(1)}, bf16[32,3,16,8,128]{4,0,3,1,2:T(8,128)(2,1)}, u32[]{:S(2)}) copy-start(bf16[32,3,16,8,128]{4,0,3,1,2:T(8,128)(2,1)} %get-tuple-element.5) | copy-start | bytes 9437188
  49.9 2.8 %copy-start.1 = (bf16[32,3,16,8,128]{4,0,3,1,2:T(8,128)(2,1)S(1)}, bf16[32,3,16,8,128]{4,0,3,1,2:T(8,128)(2,1)}, u32[]{:S(2)}) copy-start(bf16[32,3,16,8,128]{4,0,3,1,2:T(8,128)(2,1)} %get-tuple-element.6) | copy-start | bytes 9437188
  54.6 7.2 %collective-permute-start.1 = (f32[32,32]{1,0:T(8,128)S(1)}, f32[32,32]{1,0:T(8,128)S(1)}, u32[]{:S(2)}, u32[]{:S(2)}) collective-permute-start(f32[32,32]{1,0:T(8,128)S(1)} %convolution_bitcast_fusion.3), channel_id=1, source_target_pairs={{0,16},{16,32},{32,48},{48,64},{64,80},{80,96},{96,112},{112,128},... | collective-permute-start | bytes 12296 | tf_op jit(solution)/shard_map/ppermute | solution.py:10
